TPU v7x, 256 devices: a whole 4x4x8 slice. The times are simulated.
256 devices in a mesh: rows: 32 (over y, x, core), cols: 8 (over z).
Axes of the slice: x: 4, y: 4, z: 8, core: 2. Of those that a mesh axis runs over, the one named last changes fastest.
Arguments:
- sheet: bfloat16 [16, 4096, 1024], P('cols', 'rows'), may hold values from -600 to 600
- w_in: bfloat16 [1024, 16, 384], P(None, 'cols'), may hold values from -0.1875 to 0.1875
- w_out: bfloat16 [16, 128, 1024], P('cols'), may hold values from -0.125 to 0.125
Outputs:
- mixed: bfloat16 [16, 4096, 1024], P('cols', 'rows')
All inputs are finite; a program needn't handle non-finite values.
Results may differ from a plain program's by a relative error of at most 0.0067.
Values may be sent and summed in bfloat16 or wider, within the bound.
No kernel may reach another device: no remote copies, remote signals or barrier semaphores. Data moves between devices by JAX's collectives and lax.ppermute only.
A program may use at most 128 MiB of HBM per device.

v0:
```python
import jax
import jax.numpy as jnp
from jax import lax
from jax.sharding import PartitionSpec as P


def prefix(x, axis, combine, identity):
    peers, mine = (lax.axis_size(axis), lax.axis_index(axis))
    everything = lax.all_gather(x, axis)
    start = jnp.broadcast_to(jnp.asarray(identity, x.dtype), x.shape)

    def turn(k, before):
        reached = k < mine
        new = combine(before, everything[k])
        return jnp.where(reached, new, before)

    return lax.fori_loop(0, peers, turn, start)


def head_norm(values):
    return values * lax.rsqrt(jnp.mean(values * values, axis=-1, keepdims=True) + 1e-06)


def feature_map(values):
    return jax.nn.elu(values) + 1.0


def finish_proj(proj):
    parts = [
        head_norm(proj[..., 0, :]),
        head_norm(proj[..., 1, :]),
        proj[..., 2, :],
        feature_map(proj[..., 3, :]),
        feature_map(proj[..., 4, :]),
        proj[..., 5, :],
    ]
    return jnp.stack(parts, axis=-2).astype(jnp.bfloat16)


def add_states(earlier, later):
    return earlier + later


def body(sheet, w_in, w_out):
    high = lax.Precision.HIGHEST
    width = sheet.shape[2]
    heads_here = w_in.shape[1]
    hdim = w_out.shape[1] // 2
    w_flat = w_in.reshape(width, heads_here * 6 * hdim)
    piece = lax.all_gather(sheet, "cols", axis=0, tiled=True)
    xfull = piece.astype(jnp.float32)
    normed = (xfull * lax.rsqrt(jnp.mean(xfull * xfull, axis=-1, keepdims=True) + 1e-06)).astype(
        jnp.bfloat16
    )
    proj = jnp.dot(normed.reshape(-1, width), w_flat, preferred_element_type=jnp.float32)
    proj = proj.reshape(piece.shape[0], piece.shape[1], heads_here, 6, hdim)
    projected = finish_proj(proj).reshape(piece.shape[0], piece.shape[1], heads_here * 6 * hdim)
    all_cols = projected.shape[0]
    row_count = projected.shape[1]
    parts = projected.reshape(all_cols, row_count, heads_here, 6, hdim)
    qrow, krow, vrow = (parts[:, :, :, 0], parts[:, :, :, 1], parts[:, :, :, 2])
    fq, fk, vcol = (parts[:, :, :, 3], parts[:, :, :, 4], parts[:, :, :, 5])
    scale = hdim ** (-0.5)
    score = jnp.einsum("crhd,erhd->rhce", qrow, krow, preferred_element_type=jnp.float32) * scale
    expo = jnp.exp(score)
    weights = (expo / jnp.sum(expo, axis=-1, keepdims=True)).astype(jnp.bfloat16)
    orow = jnp.einsum("rhce,erhd->crhd", weights, vrow, preferred_element_type=jnp.float32).astype(
        jnp.bfloat16
    )
    states = jnp.einsum("crhk,crhv->chkv", fk, vcol, preferred_element_type=jnp.float32)
    prior = prefix(states, "rows", add_states, jnp.zeros_like(states))
    causal = (jnp.arange(row_count)[:, None] >= jnp.arange(row_count)[None, :]).astype(jnp.float32)
    inner = jnp.einsum("cthd,cshd->chts", fq, fk, preferred_element_type=jnp.float32) * causal
    local = jnp.einsum("chts,cshv->cthv", inner, vcol.astype(jnp.float32), precision=high)
    carried = jnp.einsum("cthk,chkv->cthv", fq.astype(jnp.float32), prior, precision=high)
    ocol = head_norm(carried + local).astype(jnp.bfloat16)
    results = jnp.stack([orow, ocol], axis=3).reshape(all_cols, row_count, heads_here * 2 * hdim)
    w_local = w_out.reshape(heads_here * 2 * hdim, width)
    own_cols = all_cols // lax.axis_size("cols")
    flat = jnp.dot(
        results.reshape(lax.axis_size("cols") * own_cols * row_count, -1),
        w_local,
        preferred_element_type=jnp.float32,
    )
    mixed = lax.psum_scatter(
        flat.reshape(lax.axis_size("cols") * own_cols, row_count, width),
        "cols",
        scatter_dimension=0,
        tiled=True,
    )
    return mixed.astype(jnp.bfloat16)


def solution(mesh):
    return jax.shard_map(
        body,
        mesh=mesh,
        in_specs=(P("cols", "rows", None), P(None, "cols", None), P("cols", None, None)),
        out_specs=P("cols", "rows", None),
        check_vma=False,
    )
```

profile of v0, /device:TPU:1, one launch (start us, length us, event | category | flops | bytes accessed | tf_op | source)
XLA Modules:
  0.0 364.3 jit_solution(10908132423597175600)
XLA Ops:
  6.5 0.7 all-gather.4.cloned.1.call-update
  7.3 1.7 copy.70
  9.0 1.7 copy.48
  10.7 56.8 %all-gather.4.cloned.1.call-done = bf16[16,128,1024]{2,1,0:T(8,128)(2,1)} async-done(((bf16[2,128,1024]{2,1,0:T(8,128)(2,1)}), bf16[16,128,1024]{2,1,0:T(8,128)(2,1)}) %all-gather.4.cloned.1.call-update) | async-done | bytes 4194320 | tf_op jit(solution)/shard_map/all_gather | solution.py:50
  67.5 3.2 fusion
  70.8 0.2 copy-done.2
  71.0 5.0 %fusion.41 = (bf16[16,128,2,6,64]{1,4,3,2,0:T(8,128)(2,1)S(1)}, f32[16,128,2,6,64]{1,4,3,2,0:T(8,128)S(1)}) fusion(bf16[2,6,64,1024,1]{3,2,1,0,4:T(8,128)(2,1)} %bitcast.65, bf16[16,128,1024]{2,1,0:T(8,128)(2,1)S(1)} %copy-done.2, f32[16,128]{1,0:T(8,128)S(1)} %add_rsqrt_fusion), kind=kOutput, calls=%fused_computation.56 | convolution fusion | flops 3229089792 | bytes 15212544 | tf_op jit(solution)/shard_map/dot_general | solution.py:55
  76.0 2.6 copy-done.1
  78.6 1.0 copy-done.4
  79.5 1.5 fusion.26
  81.1 0.2 reduce-scatter.2.cloned.1.call-start
  81.3 1.9 multiply_reduce_fusion.1
  83.3 2.7 fusion.22
  85.9 2.5 copy.53
  88.4 2.5 copy.54
  90.9 3.3 fusion.42
  94.3 3.0 copy.55
  97.4 1.4 copy.57
  98.8 1.1 slice_bitcast_fusion.1
  99.9 2.6 copy.56
  102.5 2.9 fusion.44
  105.4 2.2 copy.58
  107.6 4.0 %fusion.35 = f32[16,2,128,128]{3,2,1,0:T(8,128)} fusion(f32[16,128,2,6,64]{1,4,3,2,0:T(8,128)} %copy-done.1), kind=kOutput, calls=%fused_computation.54 | convolution fusion | flops 69730304 | bytes 4194304 | tf_op jit(solution)/shard_map/cthd,cshd->chts/dot_general | solution.py:73
  111.6 87.5 %all-gather.6.cloned.1.call-done = f32[512,2,64,64]{3,2,1,0:T(8,128)} async-done(((f32[16,2,64,64]{3,2,1,0:T(8,128)}), f32[512,2,64,64]{3,2,1,0:T(8,128)}) %all-gather.6.cloned.1.call-update) | async-done | bytes 16777232 | tf_op jit(solution)/shard_map/all_gather | solution.py:9
  199.1 51.7 %while.14 = (s32[]{:T(128)}, f32[16,2,64,64]{3,2,1,0:T(8,128)S(1)}, s32[]{:T(128)}, f32[32,16,2,64,64]{4,3,2,1,0:T(8,128)}, s32[]{:T(128)}, /*index=5*/s32[]{:T(128)}) while((s32[]{:T(128)}, f32[16,2,64,64]{3,2,1,0:T(8,128)S(1)}, s32[]{:T(128)}, f32[32,16,2,64,64]{4,3,2,1,0:T(8,128)}, s32[]{:T(128)}, /*index=5*/s32[]{:T(128)}) %tuple.46), condition=%wide.region_5.6_spmd.clone, body=%wide.region_4.5_spmd.clone.sunk | while | flops 393220 | bytes 1572965 | solution.py:17
  199.1 1.6 add_select_fusion.2
  200.7 1.6 add_select_fusion.2
  202.3 1.6 add_select_fusion.2
  203.9 1.6 add_select_fusion.2
  205.5 1.6 add_select_fusion.2
  207.2 1.6 add_select_fusion.2
  208.8 1.6 add_select_fusion.2
  210.4 1.6 add_select_fusion.2
  212.0 1.6 add_select_fusion.2
  213.6 1.6 add_select_fusion.2
  215.2 1.6 add_select_fusion.2
  216.9 1.6 add_select_fusion.2
  218.5 1.6 add_select_fusion.2
  220.1 1.6 add_select_fusion.2
  221.7 1.6 add_select_fusion.2
  223.3 1.6 add_select_fusion.2
  224.9 1.6 add_select_fusion.2
  226.6 1.6 add_select_fusion.2
  228.2 1.6 add_select_fusion.2
  229.8 1.6 add_select_fusion.2
  231.4 1.6 add_select_fusion.2
  233.0 1.6 add_select_fusion.2
  234.6 1.6 add_select_fusion.2
  236.3 1.6 add_select_fusion.2
  237.9 1.6 add_select_fusion.2
  239.5 1.6 add_select_fusion.2
  241.1 1.6 add_select_fusion.2
  242.7 1.6 add_select_fusion.2
  244.3 1.6 add_select_fusion.2
  246.0 1.6 add_select_fusion.2
  247.6 1.6 add_select_fusion.2
  249.2 1.6 add_select_fusion.2
  250.8 2.7 fusion.39
  253.5 3.3 multiply_reduce_fusion
  256.8 0.1 fusion.23
  257.0 0.1 pad_maximum_fusion
  257.2 4.5 %fusion.43 = f32[16,128,1024]{2,1,0:T(8,128)} fusion(bf16[16,128,256]{1,2,0:T(8,128)(2,1)S(1)} %bitcast.62, bf16[256,1024,1]{1,0,2:T(8,128)(2,1)S(1)} %bitcast.60), kind=kOutput, calls=%fused_computation.58 | convolution fusion | flops 1073741824 | bytes 9961472 | tf_op jit(solution)/shard_map/dot_general | solution.py:80
  261.7 94.0 %reduce-scatter.2.cloned.1.call-done = f32[2,128,1024]{2,1,0:T(8,128)} async-done(((f32[16,128,1024]{2,1,0:T(8,128)}), f32[2,128,1024]{2,1,0:T(8,128)}) %reduce-scatter.2.cloned.1.call-update) | async-done | bytes 1048592 | tf_op jit(solution)/shard_map/reduce_scatter | solution.py:85
  355.7 2.1 convert_element_type.38
  (22 shorter events, 0.4 us)
Async XLA Ops:
  6.5 250.6 %copy-start = (bf16[2,128,1024]{2,1,0:T(8,128)(2,1)S(1)}, bf16[2,128,1024]{2,1,0:T(8,128)(2,1)}, u32[]{:S(2)}) copy-start(bf16[2,128,1024]{2,1,0:T(8,128)(2,1)} %param.7) | copy-start | bytes 1572868
  6.5 61.0 %all-gather.4.cloned.1.call-start = ((), (), s32[]{:S(2)}) async-start(), calls=%async_computation.1 | async-start | bytes 4718592 | tf_op jit(solution)/shard_map/all_gather | solution.py:50
  7.3 191.8 %all-gather.6.cloned.1.call-start = ((), (), s32[]{:S(2)}) async-start(), calls=%async_computation.3 | async-start | bytes 34603008 | tf_op jit(solution)/shard_map/all_gather | solution.py:9
  67.5 3.4 copy-start.2
  76.0 2.6 copy-start.1
  76.0 3.6 copy-start.4
  81.1 274.6 %reduce-scatter.2.cloned.1.call-start = ((), (), s32[]{:S(2)}) async-start(), calls=%async_computation.2 | async-start | bytes 9437184 | tf_op jit(solution)/shard_map/reduce_scatter | solution.py:85
  250.8 2.7 copy-start.3
Sparse Core Ops, SparseCore 0:
  9.1 58.3 all-gather.3
  81.2 117.8 all-gather.5
  261.8 93.8 reduce-scatter.1
where the time goes:
time: 366 us; the launch traced here: 364 us
  waiting for transfers between devices  239 us (65%)
  other arithmetic  61.2 us (17%)
  matrix products  27.2 us (7%)
  local copies, waits for them, and re-layouts  22.5 us (6%)
  between operations  13.3 us (4%)
    reduce_scatter x1, waiting for transfers between devices, body(): lax.psum_scatter(flat.reshape(lax.axis_size('cols') * own_cols, row_count...  94 us
    all_gather x1, waiting for transfers between devices, prefix(): everything = lax.all_gather(x, axis)  87.5 us
    all_gather x1, waiting for transfers between devices, body(): piece = lax.all_gather(sheet, 'cols', axis=0, tiled=True)  56.8 us
    select_n x32, other arithmetic, turn(): return jnp.where(reached, new, before)  50.9 us
    squeeze x4, local copies, waits for them, and re-layouts, body(): qrow, krow, vrow = (parts[:, :, :, 0], parts[:, :, :, 1], parts[:, :, :, 2])  8.62 us
  transfers between devices with their start and end apart: 3, of which 3 were waited for; matrix products, arithmetic and copies ran while one was open for 9% of the time, Pallas kernels for 0%

commit v1 on v0

v1 whole, which is shorter than its diff:
```python
import jax
import jax.numpy as jnp
import numpy as np
from jax import lax
from jax.sharding import Mesh, PartitionSpec as P

ROWS_AXES = ("y", "x", "core")


def head_norm(values):
    return values * lax.rsqrt(jnp.mean(values * values, axis=-1, keepdims=True) + 1e-06)


def feature_map(values):
    return jax.nn.elu(values) + 1.0


def finish_proj(proj):
    parts = [
        head_norm(proj[..., 0, :]),
        head_norm(proj[..., 1, :]),
        proj[..., 2, :],
        feature_map(proj[..., 3, :]),
        feature_map(proj[..., 4, :]),
        proj[..., 5, :],
    ]
    return jnp.stack(parts, axis=-2).astype(jnp.bfloat16)


def masked_prefix(gathered, mine):
    idx = lax.broadcasted_iota(jnp.int32, gathered.shape, 0)
    before = jnp.sum(jnp.where(idx < mine, gathered, 0.0), axis=0)
    return before, jnp.sum(gathered, axis=0)


def exclusive_rows_scan(states):
    core = lax.axis_index("core")
    pair = lax.all_gather(states, "core")
    total = pair[0] + pair[1]
    own = jnp.where(core == 1, pair[0], jnp.zeros_like(pair[0]))
    half = total.shape[0] // 2
    mine = lax.dynamic_slice_in_dim(total, core * half, half, axis=0)
    gx = lax.all_gather(mine, "x")
    xpre, xsum = masked_prefix(gx, lax.axis_index("x"))
    gy = lax.all_gather(xsum, "y")
    ypre, _ = masked_prefix(gy, lax.axis_index("y"))
    chip_prefix = lax.all_gather(ypre + xpre, "core", axis=0, tiled=True)
    return chip_prefix + own


def body(sheet, w_in, w_out):
    high = lax.Precision.HIGHEST
    width = sheet.shape[2]
    heads_here = w_in.shape[1]
    hdim = w_out.shape[1] // 2
    ncols = lax.axis_size("cols")
    core = lax.axis_index("core")

    wh = width // 2
    w_part = lax.dynamic_slice_in_dim(w_out, core * wh, wh, axis=2)
    w_part = lax.all_gather(w_part, "cols", axis=0, tiled=True)
    w_full = lax.all_gather(w_part, "core", axis=2, tiled=True)

    xloc = sheet.astype(jnp.float32)
    normed = (xloc * lax.rsqrt(jnp.mean(xloc * xloc, axis=-1, keepdims=True) + 1e-06)).astype(jnp.bfloat16)
    piece = lax.all_gather(normed, "cols", axis=0, tiled=True)

    w_flat = w_in.reshape(width, heads_here * 6 * hdim)
    proj = jnp.dot(piece.reshape(-1, width), w_flat, preferred_element_type=jnp.float32)
    all_cols, row_count = piece.shape[0], piece.shape[1]
    parts = finish_proj(proj.reshape(all_cols, row_count, heads_here, 6, hdim))
    qrow, krow, vrow = (parts[:, :, :, 0], parts[:, :, :, 1], parts[:, :, :, 2])
    fq, fk, vcol = (parts[:, :, :, 3], parts[:, :, :, 4], parts[:, :, :, 5])

    states = jnp.einsum("crhk,crhv->chkv", fk, vcol, preferred_element_type=jnp.float32)
    prior = exclusive_rows_scan(states)

    scale = hdim ** (-0.5)
    score = jnp.einsum("crhd,erhd->rhce", qrow, krow, preferred_element_type=jnp.float32) * scale
    expo = jnp.exp(score)
    weights = (expo / jnp.sum(expo, axis=-1, keepdims=True)).astype(jnp.bfloat16)
    orow = jnp.einsum("rhce,erhd->crhd", weights, vrow, preferred_element_type=jnp.float32).astype(jnp.bfloat16)

    causal = (jnp.arange(row_count)[:, None] >= jnp.arange(row_count)[None, :]).astype(jnp.float32)
    inner = jnp.einsum("cthd,cshd->chts", fq, fk, preferred_element_type=jnp.float32) * causal
    local = jnp.einsum("chts,cshv->cthv", inner, vcol.astype(jnp.float32), precision=high)
    carried = jnp.einsum("cthk,chkv->cthv", fq.astype(jnp.float32), prior, precision=high)
    ocol = head_norm(carried + local).astype(jnp.bfloat16)

    results = jnp.concatenate([orow, ocol], axis=3)
    mine = lax.all_to_all(results, "cols", 0, 2, tiled=True)
    own_cols = mine.shape[0]
    mixed = jnp.dot(
        mine.reshape(own_cols * row_count, -1),
        w_full.reshape(-1, width),
        preferred_element_type=jnp.float32,
    )
    return mixed.reshape(own_cols, row_count, width).astype(jnp.bfloat16)


def split_mesh(mesh):
    devs = mesh.devices
    n_rows, n_cols = devs.shape
    try:
        nx = len({d.coords[0] for d in devs.flat})
    except Exception:
        nx = 4
    ny = n_rows // (nx * 2)
    return Mesh(devs.reshape(ny, nx, 2, n_cols), ROWS_AXES + ("cols",))


def solution(mesh):
    m4 = split_mesh(mesh)
    spec = P("cols", ROWS_AXES, None)
    return jax.shard_map(
        body,
        mesh=m4,
        in_specs=(spec, P(None, "cols", None), P("cols", None, None)),
        out_specs=spec,
        check_vma=False,
    )
```

time: 366 us -> 268 us (0.73)
  waiting for transfers between devices: 239 us -> 152 us
  other arithmetic: 61.2 us -> 13.4 us
  blocking collectives: 0 us -> 37.9 us
    reduce_scatter x1 -> x0, waiting for transfers between devices: 94 us -> none  [body(): lax.psum_scatter(flat.reshape(lax.axis_size('cols') * own_cols, row_count...]
    select_n x32 -> x0, other arithmetic: 50.9 us -> none  [turn(): return jnp.where(reached, new, before)]
    all_to_all x0 -> x1, blocking collectives: none -> 34.5 us  [body(): mine = lax.all_to_all(results, 'cols', 0, 2, tiled=True)]
    all_gather x2 -> x6, waiting for transfers between devices: 144 us -> 152 us  [the longest x1 55.1 us: body(): piece = lax.all_gather(normed, 'cols', axis=0, tiled=True)]
  transfers between devices with their start and end apart: 3 -> 6, of which waited for: 3 -> 5; matrix products, arithmetic and copies ran while one was open for 9% -> 16% of each run, Pallas kernels for 0% -> 0%
where the time goes in v1:
time: 268 us; the launch traced here: 267 us
  waiting for transfers between devices  152 us (57%)
  blocking collectives  37.9 us (14%)
  local copies, waits for them, and re-layouts  25.3 us (9%)
  matrix products  23.9 us (9%)
  between operations  13.8 us (5%)
  other arithmetic  13.4 us (5%)
    all_gather x1, waiting for transfers between devices, body(): piece = lax.all_gather(normed, 'cols', axis=0, tiled=True)  55.1 us
    all_gather x1, waiting for transfers between devices, body(): w_part = lax.all_gather(w_part, 'cols', axis=0, tiled=True)  35.2 us
    all_to_all x1, blocking collectives, body(): mine = lax.all_to_all(results, 'cols', 0, 2, tiled=True)  34.5 us
    all_gather x1, waiting for transfers between devices, exclusive_rows_scan(): gx = lax.all_gather(mine, 'x')  33 us
    all_gather x1, waiting for transfers between devices, exclusive_rows_scan(): pair = lax.all_gather(states, 'core')  15.5 us
    all_gather x1, waiting for transfers between devices, exclusive_rows_scan(): gy = lax.all_gather(xsum, 'y')  13.6 us
    squeeze x4, local copies, waits for them, and re-layouts, body(): qrow, krow, vrow = (parts[:, :, :, 0], parts[:, :, :, 1], parts[:, :, :, 2])  7.74 us
    dot_general x1, matrix products, body(): jnp.dot(piece.reshape(-1, width), w_flat, preferred_element_type=jnp.floa...  5.78 us
  transfers between devices with their start and end apart: 6, of which 5 were waited for; matrix products, arithmetic and copies ran while one was open for 16% of the time, Pallas kernels for 0%

profile of v1, /device:TPU:1, one launch (start us, length us, event | category | flops | bytes accessed | tf_op | source)
XLA Modules:
  0.0 267.2 jit_solution(8593396329968372122)
XLA Ops:
  6.5 1.3 fusion.10
  7.8 2.0 fusion.11
  9.8 0.0 all-gather.10.cloned.1.call-update
  9.8 0.0 all-gather.16.cloned.1.call-start
  9.9 1.7 copy.59
  11.6 1.6 copy.38
  13.3 55.1 %all-gather.10.cloned.1.call-done = bf16[16,128,1024]{2,1,0:T(8,128)(2,1)} async-done(((bf16[2,128,1024]{2,1,0:T(8,128)(2,1)}), bf16[16,128,1024]{2,1,0:T(8,128)(2,1)}) %all-gather.10.cloned.1.call-update) | async-done | bytes 4194320 | tf_op jit(solution)/shard_map/all_gather | solution.py:66
  68.4 5.8 %fusion.43 = (bf16[16,128,2,6,64]{1,4,3,2,0:T(8,128)(2,1)S(1)}, f32[16,128,2,6,64]{1,4,3,2,0:T(8,128)S(1)}) fusion(bf16[2,6,64,1024,1]{3,2,1,0,4:T(8,128)(2,1)} %bitcast.62, bf16[16,128,1024]{2,1,0:T(8,128)(2,1)} %all-gather.10.cloned.1.call-done), kind=kOutput, calls=%fused_computation.67 | convolution fusion | flops 3222798336 | bytes 15204352 | tf_op jit(solution)/shard_map/dot_general | solution.py:69
  74.2 0.0 copy-start.2
  74.2 0.0 copy-start.5
  74.2 2.6 copy-done.2
  76.8 1.0 copy-done.5
  77.8 1.5 fusion.26
  79.3 0.0 all-gather.16.cloned.1.call-update
  79.4 0.0 all-gather.20.cloned.1.call-start
  79.4 15.5 %all-gather.16.cloned.1.call-done = f32[32,2,64,64]{3,2,1,0:T(8,128)} async-done(((f32[16,2,64,64]{3,2,1,0:T(8,128)}), f32[32,2,64,64]{3,2,1,0:T(8,128)}) %all-gather.16.cloned.1.call-update) | async-done | bytes 1048592 | tf_op jit(solution)/shard_map/all_gather | solution.py:38
  94.9 1.7 fusion.42
  96.6 0.9 dynamic-slice_add_fusion
  97.5 0.0 all-gather.20.cloned.1.call-update
  97.5 0.0 all-gather.12.cloned.1.call-start
  97.5 0.0 copy-done
  97.5 0.8 constant_dynamic-slice_fusion
  98.3 0.0 all-gather.12.cloned.1.call-update
  98.3 0.0 all-gather.18.cloned.1.call-start
  98.4 33.0 %all-gather.20.cloned.1.call-done = f32[32,2,64,64]{3,2,1,0:T(8,128)} async-done(((f32[8,2,64,64]{3,2,1,0:T(8,128)}), f32[32,2,64,64]{3,2,1,0:T(8,128)}) %all-gather.20.cloned.1.call-update) | async-done | bytes 1048592 | tf_op jit(solution)/shard_map/all_gather | solution.py:43
  131.3 3.1 %select_reduce_fusion = (f32[8,2,64,64]{3,2,1,0:T(8,128)}, f32[8,2,64,64]{3,2,1,0:T(8,128)}) fusion(f32[4,8,2,64,64]{4,3,2,1,0:T(8,128)} %bitcast.59, pred[4]{0:T(512)(128)(4,1)S(1)} %iota_compare_fusion.1), kind=kLoop, calls=%fused_computation.8 | loop fusion | flops 655360 | bytes 1572868 | tf_op jit(solution)/shard_map/reduce_sum | solution.py:32
  134.4 0.0 all-gather.18.cloned.1.call-update
  134.4 0.2 all-gather.14.cloned.1.call-start
  134.7 35.2 %all-gather.12.cloned.1.call-done = bf16[16,128,512]{2,1,0:T(8,128)(2,1)} async-done(((bf16[2,128,512]{2,1,0:T(8,128)(2,1)}), bf16[16,128,512]{2,1,0:T(8,128)(2,1)}) %all-gather.12.cloned.1.call-update) | async-done | bytes 2097168 | tf_op jit(solution)/shard_map/all_gather | solution.py:61
  169.9 0.0 all-gather.14.cloned.1.call-update
  169.9 1.9 multiply_reduce_fusion.1
  171.8 1.1 slice_bitcast_fusion.1
  173.0 1.9 fusion.21
  174.9 2.5 copy.43
  177.4 2.5 copy.44
  179.9 2.2 fusion.44
  182.1 1.3 copy.45
  183.5 0.1 fusion.27
  183.5 0.1 divide_convert_fusion
  183.6 1.4 copy.47
  185.0 1.6 copy.46
  186.7 1.7 fusion.45
  188.3 3.0 %copy.48 = bf16[128,2,64,16]{0,2,1,3:T(8,128)(2,1)} copy(bf16[128,2,64,16]{2,3,1,0:T(8,128)(2,1)} %fusion.45) | data formatting | bytes 1048576 | tf_op jit(solution)/shard_map/rhce,erhd->crhd/dot_general | solution.py:82
  191.3 2.6 fusion.37
  193.9 0.0 copy-start.3
  193.9 13.6 %all-gather.18.cloned.1.call-done = f32[32,2,64,64]{3,2,1,0:T(8,128)} async-done(((f32[8,2,64,64]{3,2,1,0:T(8,128)}), f32[32,2,64,64]{3,2,1,0:T(8,128)}) %all-gather.18.cloned.1.call-update) | async-done | bytes 1048592 | tf_op jit(solution)/shard_map/all_gather | solution.py:45
  207.5 2.0 select_reduce_fusion.1
  209.5 0.0 copy-start.1
  209.5 0.0 copy-done.3
  209.5 0.1 add.72
  209.6 3.4 %all_gather.34 = f32[16,2,64,64]{3,2,1,0:T(8,128)S(1)} all-gather(f32[8,2,64,64]{3,2,1,0:T(8,128)S(1)} %add.72), channel_id=1, replica_groups=mesh['y'=4,'x'=4,'core'=2,'cols'=8] {'core'}, dimensions={0}, use_global_device_ids=true | all-gather | bytes 786432 | tf_op jit(solution)/shard_map/all_gather | solution.py:47
  213.0 0.0 copy-done.1
  213.0 2.6 fusion.18
  215.6 0.0 copy-start.4
  215.6 3.3 %multiply_reduce_fusion = (f32[16,128,2]{1,2,0:T(2,128)S(1)}, f32[16,128,2,64]{1,3,2,0:T(8,128)S(1)}) fusion(f32[16,2,64,128]{3,2,1,0:T(8,128)S(1)} %fusion.18, f32[16,2,128,128]{3,2,1,0:T(8,128)S(1)} %fusion.37, f32[128,128]{1,0:T(8,128)S(1)} %fusion.28, bf16[16,128,2,6,64]{1,4,3,2,0:T(8,128)(2,1)} %copy-done.5), kind=kOutput, calls=%fused_computation.28 | convolution fusion | flops 403959808 | bytes 4800512 | tf_op jit(solution)/shard_map/chts,cshv->cthv/dot_general | solution.py:86
  218.9 0.1 multiply_convert_fusion
  219.1 0.0 copy-done.4
  219.1 0.1 pad_maximum_fusion
  219.2 0.8 copy.53
  220.0 34.5 %all_to_all.15 = bf16[16,128,2,128]{3,2,1,0:T(2,128)(2,1)S(1)} all-to-all(bf16[16,128,2,128]{3,2,1,0:T(2,128)(2,1)S(1)} %copy.53), channel_id=1, replica_groups=mesh['y'=4,'x'=4,'core'=2,'cols'=8] {'cols'}, dimensions={0} | all-to-all | bytes 2097152 | tf_op jit(solution)/shard_map/all_to_all | solution.py:91
  254.5 0.7 copy.76
  255.2 0.8 dot_general.39
  256.0 0.0 all-gather.14.cloned.1.call-done
  256.1 4.2 %convolution_convert_fusion = bf16[2,128,1024]{2,1,0:T(8,128)(2,1)} fusion(bf16[2,128,2048]{2,1,0:T(8,128)(2,1)S(1)} %dot_general.39, bf16[2048,1024,1]{1,0,2:T(8,128)(2,1)} %bitcast.63), kind=kOutput, calls=%fused_computation.14 | convolution fusion | flops 1074003968 | bytes 5767168 | tf_op jit(solution)/shard_map/dot_general | solution.py:93
  (11 shorter events, 0.1 us)
Async XLA Ops:
  6.5 91.0 %copy-start = (bf16[2,128,1024]{2,1,0:T(8,128)(2,1)S(1)}, bf16[2,128,1024]{2,1,0:T(8,128)(2,1)}, u32[]{:S(2)}) copy-start(bf16[2,128,1024]{2,1,0:T(8,128)(2,1)} %param.5) | copy-start | bytes 1572868
  6.5 61.8 %all-gather.10.cloned.1.call-start = ((), (), s32[]{:S(2)}) async-start(), calls=%async_computation.1 | async-start | bytes 4718592 | tf_op jit(solution)/shard_map/all_gather | solution.py:66
  9.8 85.1 %all-gather.16.cloned.1.call-start = ((), (), s32[]{:S(2)}) async-start(), calls=%async_computation.4 | async-start | bytes 3145728 | tf_op jit(solution)/shard_map/all_gather | solution.py:38
  74.2 2.7 copy-start.2
  74.2 3.6 %copy-start.5 = (bf16[16,128,2,6,64]{1,4,3,2,0:T(8,128)(2,1)}, bf16[16,128,2,6,64]{1,4,3,2,0:T(8,128)(2,1)S(1)}, u32[]{:S(2)}) copy-start(bf16[16,128,2,6,64]{1,4,3,2,0:T(8,128)(2,1)S(1)} %get-tuple-element.13) | copy-start | bytes 9437188
  79.4 52.0 %all-gather.20.cloned.1.call-start = ((), (), s32[]{:S(2)}) async-start(), calls=%async_computation.6 | async-start | bytes 2621440 | tf_op jit(solution)/shard_map/all_gather | solution.py:43
  97.5 72.4 %all-gather.12.cloned.1.call-start = ((), (), s32[]{:S(2)}) async-start(), calls=%async_computation.2 | async-start | bytes 2359296 | tf_op jit(solution)/shard_map/all_gather | solution.py:61
  98.3 109.2 %all-gather.18.cloned.1.call-start = ((), (), s32[]{:S(2)}) async-start(), calls=%async_computation.5 | async-start | bytes 2621440 | tf_op jit(solution)/shard_map/all_gather | solution.py:45
  134.4 121.6 %all-gather.14.cloned.1.call-start = ((), (), s32[]{:S(2)}) async-start(), calls=%async_computation.3 | async-start | bytes 6291456 | tf_op jit(solution)/shard_map/all_gather | solution.py:62
  193.9 15.6 %copy-start.3 = (f32[8,2,64,64]{3,2,1,0:T(8,128)S(1)}, f32[8,2,64,64]{3,2,1,0:T(8,128)}, u32[]{:S(2)}) copy-start(f32[8,2,64,64]{3,2,1,0:T(8,128)} %get-tuple-element.7) | copy-start | bytes 786436
  209.5 3.5 %copy-start.1 = (f32[32,2,64,64]{3,2,1,0:T(8,128)S(1)}, f32[32,2,64,64]{3,2,1,0:T(8,128)}, u32[]{:S(2)}) copy-start(f32[32,2,64,64]{3,2,1,0:T(8,128)} %all-gather.16.cloned.1.call-done) | copy-start | bytes 3145732
  215.6 3.5 %copy-start.4 = (bf16[128,2,64,16]{0,2,1,3:T(8,128)(2,1)S(1)}, bf16[128,2,64,16]{0,2,1,3:T(8,128)(2,1)}, u32[]{:S(2)}) copy-start(bf16[128,2,64,16]{0,2,1,3:T(8,128)(2,1)} %copy.48) | copy-start | bytes 1572868
Sparse Core Ops, SparseCore 0:
  10.0 58.3 all-gather.9
  79.5 15.3 all-gather.15
  97.6 33.6 all-gather.19
  133.0 36.8 all-gather.11
  171.6 35.9 all-gather.17
  209.2 19.9 all-gather.13
